TPU v7x, 32 devices: a whole 2x2x4 slice. The times are simulated.
32 devices in a mesh: seq: 16 (over z, x, core), head: 2 (over y).
Axes of the slice: x: 2, y: 2, z: 4, core: 2. Of those that a mesh axis runs over, the one named last changes fastest.
Arguments:
- step_tokens: bfloat16 [2, 12, 8, 2560], P(None, None, None, 'head'), may hold values from -6 to 6
- parents: int32 [2, 12, 8], replicated, may hold values from 0 to 7
- tail_cache: bfloat16 [12, 8, 64, 2048], P(None, 'head', 'seq'), may hold values from -192 to 192
- tail_len: int32 [12], replicated, may hold values from 0 to 62, as said below
- cache: bfloat16 [8, 2048, 2048], P(None, ('seq', 'head')), may hold values from -192 to 192
- cache_len: int32 [8], replicated, may hold values from 256 to 2048, as said below
- prompt_states: bfloat16 [4, 128, 2560], P(None, 'seq', 'head'), may hold values from -6 to 6
- prompt_len: int32 [4], replicated, may hold values from 32 to 128, as said below
- in_gain: float32 [2560], P('head'), may hold values from 0.5 to 1.5
- w_query: bfloat16 [2560, 2048], P('head', 'seq'), may hold values from -0.125 to 0.125
- w_keyval: bfloat16 [2560, 2048], P('head', 'seq'), may hold values from -0.125 to 0.125
- q_gain: float32 [256], replicated, may hold values from 0.6 to 32
- k_gain: float32 [256], replicated, may hold values from 0.6 to 32
- w_out: bfloat16 [2048, 2560], P('seq', 'head'), may hold values from -0.125 to 0.125
- post_gain: float32 [2560], P('head'), may hold values from 0.5 to 1.5
- ffn_gain: float32 [2560], P('head'), may hold values from 0.5 to 1.5
- w_gate: bfloat16 [2560, 10240], P('head', 'seq'), may hold values from -0.125 to 0.125
- w_up: bfloat16 [2560, 10240], P('head', 'seq'), may hold values from -0.125 to 0.125
- w_down: bfloat16 [10240, 2560], P('seq', 'head'), may hold values from -0.0625 to 0.0625
- final_gain: float32 [2560], P('head'), may hold values from 0.5 to 1.5
Outputs:
- decoded: bfloat16 [2, 12, 8, 2560], P(None, None, None, 'head')
Inputs may be any that keep to these rules, and one draw needn't show every extreme that they name: `tail_len`: the first 4 groups have 0; the largest entry is exactly 62. `cache_len`: the largest entry is exactly 2048. `prompt_len`: the largest entry is exactly 128.
All inputs are finite; a program needn't handle non-finite values.
Results may differ from a plain program's by a relative error of at most 0.0055.
The roundings to bfloat16 on the way count: a program that leaves them out, or rounds other values in their place, can miss the bound.
Values may be sent and summed in bfloat16 or wider, within the bound.
No kernel may reach another device: no remote copies, remote signals or barrier semaphores. Data moves between devices by JAX's collectives and lax.ppermute only.
A program may use at most 128 MiB of HBM per device.

v0:
```python
import jax
import jax.numpy as jnp
from jax import lax
from jax.sharding import PartitionSpec as P

D = 2560
QH = 8
KVH = 4
HD = 256
QD = 2048
EPS = 1e-06
NEG = -1e30
QSCALE = 0.0625


def norm_heads(values, gain, scale):
    shaped = values.reshape(values.shape[:-1] + (-1, gain.shape[0]))
    shaped = shaped * lax.rsqrt(jnp.mean(shaped * shaped, -1, keepdims=True) + EPS) * gain * scale
    return shaped.reshape(values.shape)


def finish_keys(pairs, k_gain):
    half = pairs.shape[-1] // 2
    keys = norm_heads(pairs[..., :half], k_gain, 1.0)
    return jnp.concatenate([keys, pairs[..., half:]], -1).astype(jnp.bfloat16)


def split_pairs(pairs):
    half = pairs.shape[-1] // 2
    keys = pairs[..., :half].reshape(pairs.shape[:-1] + (KVH, HD))
    values = pairs[..., half:].reshape(pairs.shape[:-1] + (KVH, HD))
    return (keys, values)


def project_tokens(tokens, in_gain, w_query, w_keyval, q_gain, k_gain):
    flat = tokens.reshape(-1, tokens.shape[-1]).astype(jnp.float32)
    scaled = (flat * in_gain).astype(jnp.bfloat16)
    q_part = jnp.dot(scaled, w_query, preferred_element_type=jnp.float32)
    kv_part = jnp.dot(scaled, w_keyval, preferred_element_type=jnp.float32)
    squares = jnp.sum(flat * flat, -1)
    q_part, kv_part, squares = lax.psum((q_part, kv_part, squares), "head")
    factor = lax.rsqrt(squares / D + EPS)[:, None]
    q_raw = (q_part * factor).astype(jnp.bfloat16)
    kv_raw = (kv_part * factor).astype(jnp.bfloat16)
    q_raw, kv_raw = (
        lax.all_gather(q_raw, "seq", axis=1, tiled=True),
        lax.all_gather(kv_raw, "seq", axis=1, tiled=True),
    )
    queries = norm_heads(q_raw.astype(jnp.float32), q_gain, QSCALE).astype(jnp.bfloat16)
    fresh = finish_keys(kv_raw.astype(jnp.float32), k_gain)
    return (queries, fresh)


def shards(
    step_tokens,
    parents,
    tail_cache,
    tail_len,
    cache,
    cache_len,
    prompt_states,
    prompt_len,
    in_gain,
    w_query,
    w_keyval,
    q_gain,
    k_gain,
    w_out,
    post_gain,
    ffn_gain,
    w_gate,
    w_up,
    w_down,
    final_gain,
):
    f32 = jnp.float32
    bf16 = jnp.bfloat16
    n_head = lax.axis_size("head")
    n_seq = lax.axis_size("seq")
    seq_at = lax.axis_index("seq")
    head_at = lax.axis_index("head")
    flat_at = seq_at * n_head + head_at
    steps, groups, beams, width = step_tokens.shape
    pre = prompt_states.shape[0]
    repeat = QH // KVH
    col_block = QD // n_seq
    block_head = jnp.arange(n_seq) * col_block // HD
    head_pick = (jnp.arange(QH)[:, None] == block_head[None, :]).astype(f32)
    rows = jnp.transpose(prompt_states, (1, 0, 2)).astype(f32)
    prompt_scaled = (rows * in_gain).astype(bf16).reshape(-1, width)
    prompt_squares = jnp.sum(rows * rows, -1).reshape(-1)
    prompt_terms = jnp.dot(
        prompt_scaled,
        lax.all_gather(w_keyval, "seq", axis=1, tiled=True),
        preferred_element_type=f32,
    )
    prompt_sum, prompt_sq = (
        lax.psum_scatter(prompt_terms, "head", scatter_dimension=0, tiled=True),
        lax.psum_scatter(prompt_squares, "head", scatter_dimension=0, tiled=True),
    )
    prompt_pairs = finish_keys(prompt_sum * lax.rsqrt(prompt_sq / D + EPS)[:, None], k_gain)
    prompt_seg = prompt_pairs.shape[0] // pre
    prompt_pairs = jnp.transpose(prompt_pairs.reshape(prompt_seg, pre, -1), (1, 0, 2))
    prompt_keys, prompt_values = split_pairs(prompt_pairs)
    prompt_ok = (flat_at * prompt_seg + jnp.arange(prompt_seg))[None, :] < prompt_len[:, None]
    cache_seg = cache.shape[1]
    cache_keys, cache_values = split_pairs(cache)
    cache_ok = (flat_at * cache_seg + jnp.arange(cache_seg))[None, :] < cache_len[:, None]
    tail_seg = tail_cache.shape[2]
    local_beams = tail_cache.shape[1]
    beam_ids = head_at * local_beams + jnp.arange(local_beams)
    offset = (seq_at * tail_seg + jnp.arange(tail_seg))[None, :] - tail_len[:, None]
    all_beams = jnp.arange(beams)
    every_query, every_fresh = project_tokens(
        step_tokens, in_gain, w_query, w_keyval, q_gain, k_gain
    )
    every_query = every_query.reshape(steps, groups, beams, -1)
    every_fresh = every_fresh.reshape(steps, groups, beams, -1)
    tail_state = tail_cache
    decoded = []
    for step in range(steps):
        query = every_query[step]
        new_pairs = every_fresh[step]
        everyone = lax.all_gather(tail_state, "head", axis=1, tiled=True)
        picks = lax.dynamic_slice_in_dim(parents[step], head_at * local_beams, local_beams, 1)
        tail_state = jnp.take_along_axis(everyone, picks[:, :, None, None], axis=1)
        owner = jnp.broadcast_to(all_beams[None, :, None], (groups, beams, tail_seg))
        mine = lax.dynamic_slice_in_dim(new_pairs, head_at * local_beams, local_beams, 1)
        tail_state = jnp.where((offset == step)[:, None, :, None], mine[:, :, None, :], tail_state)
        tail_ok = (offset <= step)[:, None, None, :] & (
            owner[:, :, None, :] == beam_ids[None, None, :, None]
        )
        shaped = query.reshape(groups, beams, KVH, repeat, HD)
        tail_keys, tail_values = split_pairs(tail_state)
        pre_scores = jnp.einsum(
            "gbkrd,gtkd->gbkrt", shaped[:pre], prompt_keys, preferred_element_type=f32
        )
        dec_scores = jnp.einsum(
            "gbkrd,gtkd->gbkrt", shaped[pre:], cache_keys, preferred_element_type=f32
        )
        tail_scores = jnp.einsum(
            "gbkrd,gctkd->gbkrct", shaped, tail_keys, preferred_element_type=f32
        )
        pre_mask = prompt_ok[:, None, None, None, :]
        dec_mask = cache_ok[:, None, None, None, :]
        tail_mask = tail_ok[:, :, None, None, :, :]
        pre_scores = jnp.where(pre_mask, pre_scores, NEG)
        dec_scores = jnp.where(dec_mask, dec_scores, NEG)
        tail_scores = jnp.where(tail_mask, tail_scores, NEG)
        top = jnp.concatenate([jnp.max(pre_scores, -1), jnp.max(dec_scores, -1)], 0)
        top = jnp.maximum(top, jnp.max(tail_scores, (-2, -1)))
        top = lax.pmax(top, ("seq", "head"))
        pre_weights = jnp.where(pre_mask, jnp.exp(pre_scores - top[:pre, ..., None]), 0.0)
        dec_weights = jnp.where(dec_mask, jnp.exp(dec_scores - top[pre:, ..., None]), 0.0)
        tail_weights = jnp.where(tail_mask, jnp.exp(tail_scores - top[..., None, None]), 0.0)
        total = jnp.concatenate([jnp.sum(pre_weights, -1), jnp.sum(dec_weights, -1)], 0)
        total = total + jnp.sum(tail_weights, (-2, -1))
        weighted = jnp.concatenate(
            [
                jnp.einsum(
                    "gbkrt,gtkd->gbkrd",
                    pre_weights.astype(bf16),
                    prompt_values,
                    preferred_element_type=f32,
                ),
                jnp.einsum(
                    "gbkrt,gtkd->gbkrd",
                    dec_weights.astype(bf16),
                    cache_values,
                    preferred_element_type=f32,
                ),
            ],
            0,
        )
        weighted = weighted + jnp.einsum(
            "gbkrct,gctkd->gbkrd",
            tail_weights.astype(bf16),
            tail_values,
            preferred_element_type=f32,
        )
        weighted = weighted.reshape(groups * beams, -1)
        total = total.reshape(groups * beams, -1)
        spread_total = jnp.sum(total[:, :, None] * head_pick[None, :, :], 1)
        share, own_total = (
            lax.psum_scatter(weighted, "seq", scatter_dimension=1, tiled=True),
            lax.psum_scatter(spread_total, "seq", scatter_dimension=1, tiled=True),
        )
        share, own_total = lax.psum((share, own_total), "head")
        attn = (share / own_total).astype(bf16)
        partial_out = jnp.dot(attn, w_out, preferred_element_type=f32)
        out_proj = lax.psum(partial_out, "seq")
        out_sq = lax.psum(jnp.sum(out_proj * out_proj, -1), "head")
        x_f = step_tokens[step].reshape(groups * beams, -1).astype(f32)
        state = (x_f + out_proj * lax.rsqrt(out_sq / D + EPS)[:, None] * post_gain).astype(bf16)
        state = lax.optimization_barrier(state)
        state_f = state.astype(f32)
        scaled_two = (state_f * ffn_gain).astype(bf16)
        gate_part = jnp.dot(scaled_two, w_gate, preferred_element_type=f32)
        up_part = jnp.dot(scaled_two, w_up, preferred_element_type=f32)
        gate_part, up_part, state_sq = lax.psum(
            (gate_part, up_part, jnp.sum(state_f * state_f, -1)), "head"
        )
        norm_s = lax.rsqrt(state_sq / D + EPS)[:, None]
        inner = (jax.nn.gelu(gate_part * norm_s, approximate=True) * (up_part * norm_s)).astype(
            bf16
        )
        ffn_out = lax.psum(jnp.dot(inner, w_down, preferred_element_type=f32), "seq")
        ffn_sq = lax.psum(jnp.sum(ffn_out * ffn_out, -1), "head")
        result = (state_f + ffn_out * lax.rsqrt(ffn_sq / D + EPS)[:, None] * final_gain).astype(
            bf16
        )
        decoded.append(result.reshape(groups, beams, -1))
    return jnp.stack(decoded)


def solution(mesh):
    return jax.shard_map(
        shards,
        mesh=mesh,
        in_specs=(
            P(None, None, None, "head"),
            P(),
            P(None, "head", "seq", None),
            P(),
            P(None, ("seq", "head"), None),
            P(),
            P(None, "seq", "head"),
            P(),
            P("head"),
            P("head", "seq"),
            P("head", "seq"),
            P(),
            P(),
            P("seq", "head"),
            P("head"),
            P("head"),
            P("head", "seq"),
            P("head", "seq"),
            P("seq", "head"),
            P("head"),
        ),
        out_specs=P(None, None, None, "head"),
        check_vma=False,
    )
```

profile of v0, /device:TPU:0, one launch (start us, length us, event | category | flops | bytes accessed | tf_op | source)
XLA Modules:
  0.0 628.8 jit_solution(9408125753058318404)
XLA Ops:
  6.5 1.3 fusion.9
  7.9 1.9 fusion.145
  12.6 5.8 all-reduce.11
  19.1 17.0 %all-reduce.28.cloned.1.call-done = (f32[192,128]{1,0:T(8,128)}, f32[192,128]{1,0:T(8,128)}) async-done(((f32[192,128]{1,0:T(8,128)}, f32[192,128]{1,0:T(8,128)}), (f32[192,128]{1,0:T(8,128)}, f32[192,128]{1,0:T(8,128)})) %all-reduce.28.cloned.1.call-update) | async-done | bytes 196624 | tf_op jit(solution)/shard_map/psum | solution.py:41
  37.1 23.5 %all_gather.17 = bf16[192,2048]{1,0:T(8,128)(2,1)S(1)} all-gather(bf16[192,128]{1,0:T(8,128)(2,1)S(1)} %get-tuple-element.70), channel_id=1, replica_groups=mesh['seq'=16,'head'=2] {'seq'}, dimensions={1}, use_global_device_ids=true | all-gather | bytes 835584 | tf_op jit(solution)/shard_map/all_gather | solution.py:47
  62.4 1.5 mul.381
  66.4 2.9 gather_fusion
  69.4 1.7 select_select_fusion.1
  73.5 2.7 fusion.131
  76.3 1.6 reshape.377
  77.9 1.9 reshape.375
  83.1 22.2 %all_gather.16 = bf16[192,2048]{1,0:T(8,128)(2,1)S(1)} all-gather(bf16[192,128]{1,0:T(8,128)(2,1)S(1)} %get-tuple-element.71), channel_id=1, replica_groups=mesh['seq'=16,'head'=2] {'seq'}, dimensions={1}, use_global_device_ids=true | all-gather | bytes 835584 | tf_op jit(solution)/shard_map/all_gather | solution.py:46
  105.5 1.8 copy.246
  107.2 2.4 reduce_sum.180
  114.6 1.7 fusion.139
  116.4 1.7 fusion.141
  121.2 2.0 fusion.37
  124.3 4.0 gather_fusion.1
  128.3 1.9 select_select_fusion
  130.2 28.0 %all-gather.4.cloned.1.call-done = bf16[1280,2048]{1,0:T(8,128)(2,1)} async-done(((bf16[1280,128]{1,0:T(8,128)(2,1)}), bf16[1280,2048]{1,0:T(8,128)(2,1)}) %all-gather.4.cloned.1.call-update) | async-done | bytes 5242896 | tf_op jit(solution)/shard_map/all_gather | solution.py:94
  158.2 4.2 fusion.143
  164.5 2.1 fusion.34
  167.7 4.7 reduce-scatter.4.cloned.1.call-done
  173.9 1.9 fusion.142
  175.9 1.9 fusion.140
  177.9 40.8 %all-reduce.3 = (f32[12,8,4,2]{1,3,2,0:T(2,128)S(1)}, f32[12,8,4,2]{1,3,2,0:T(2,128)S(1)}) all-reduce(f32[12,8,4,2]{1,3,2,0:T(2,128)S(1)} %maximum_maximum_fusion.1, f32[12,8,4,2]{1,3,2,0:T(2,128)S(1)} %maximum_maximum_fusion), channel_id=1, replica_groups=mesh['seq'=16,'head'=2] {'seq','head'}, use_global_device_ids=true, to_apply=%region_35.37 | all-reduce | flops 1536 | bytes 12288 | tf_op jit(solution)/shard_map/pmax | solution.py:152
  220.0 1.5 fusion.27
  223.8 1.6 convolution_bitcast_fusion.3
  225.4 1.4 fusion.4
  230.1 1.6 convolution_bitcast_fusion.2
  231.7 1.4 fusion.3
  235.1 60.1 %all-reduce.4 = (f32[96,16]{0,1:T(8,128)S(1)}, f32[96,16]{0,1:T(8,128)S(1)}) all-reduce(f32[96,16]{0,1:T(8,128)S(1)} %get-tuple-element.7, f32[96,16]{0,1:T(8,128)S(1)} %get-tuple-element.6), channel_id=7, replica_groups=mesh['seq'=16,'head'=2] {'seq'}, use_global_device_ids=true, to_apply=%region_42.44.clone | all-reduce | flops 3072 | bytes 24576
  295.2 1.2 fusion.116
  296.4 1.2 fusion.115
  297.6 45.9 %reduce-scatter.8.cloned.1.call-done = f32[96,128]{1,0:T(8,128)} async-done(((f32[96,2048]{1,0:T(8,128)}), f32[96,128]{1,0:T(8,128)}) %reduce-scatter.8.cloned.1.call-update) | async-done | bytes 49168 | tf_op jit(solution)/shard_map/reduce_scatter | solution.py:185
  343.6 22.5 %all-reduce.24.cloned.1.call-done = (f32[96,128]{1,0:T(8,128)}, f32[96]{0:T(128)}, f32[96,128]{1,0:T(8,128)}, f32[96]{0:T(128)}) async-done(((f32[96,128]{1,0:T(8,128)}, f32[96]{0:T(128)}, f32[96,128]{1,0:T(8,128)}, f32[96]{0:T(128)}), (f32[96,128]{1,0:T(8,128)}, f32[96]{0:T(128)}, f32[96,128]{1,0:T(8,128)}, f32[96]{0:T(128)})) %all-reduce.24.cloned.1.call-update) | async-done | bytes 99088 | tf_op jit(solution)/shard_map/psum | solution.py:188
  366.1 1.9 fusion.111
  367.9 1.9 fusion.110
  369.9 94.0 %all-reduce.22.cloned.1.call-done = (f32[96,1280]{1,0:T(8,128)}, f32[96,1280]{1,0:T(8,128)}) async-done(((f32[96,1280]{1,0:T(8,128)}, f32[96,1280]{1,0:T(8,128)}), (f32[96,1280]{1,0:T(8,128)}, f32[96,1280]{1,0:T(8,128)})) %all-reduce.22.cloned.1.call-update) | async-done | bytes 983056 | tf_op jit(solution)/shard_map/psum | solution.py:191
  466.2 4.9 all-reduce.9
  471.2 1.7 fusion.25
  477.7 4.9 all-reduce.8
  482.7 33.1 %all-reduce.26.cloned.1.call-done = (f32[96,640]{1,0:T(8,128)}, f32[96,640]{1,0:T(8,128)}, f32[96,640]{1,0:T(8,128)}, f32[96,640]{1,0:T(8,128)}) async-done(((f32[96,640]{1,0:T(8,128)}, f32[96,640]{1,0:T(8,128)}, f32[96,640]{1,0:T(8,128)}, f32[96,640]{1,0:T(8,128)}), (f32[96,640]{1,0:T(8,128)}, f32[96,640]{1,0:T(8,128)}, f32[96,640]{1,0:T(8,128)}, f32[96,640]{1,0:T(8,128)})) %all-reduce.26.cloned.1.call-update) | async-done | bytes 983056 | tf_op jit(solution)/shard_map/psum | solution.py:200
  515.7 2.4 fusion.81
  518.1 1.3 fusion.83
  519.5 93.3 %all-reduce.20.cloned.1.call-done = (f32[96,1280]{1,0:T(8,128)}, f32[96,1280]{1,0:T(8,128)}) async-done(((f32[96,1280]{1,0:T(8,128)}, f32[96,1280]{1,0:T(8,128)}), (f32[96,1280]{1,0:T(8,128)}, f32[96,1280]{1,0:T(8,128)})) %all-reduce.20.cloned.1.call-update) | async-done | bytes 983056 | tf_op jit(solution)/shard_map/psum | solution.py:207
  615.1 4.9 all-reduce.7
  620.1 1.4 fusion.58
  (258 shorter events, 46.8 us)
Async XLA Ops:
  6.5 509.2 %copy-start = (bf16[640,1280]{1,0:T(8,128)(2,1)S(1)}, bf16[640,1280]{1,0:T(8,128)(2,1)}, u32[]{:S(2)}) copy-start(bf16[640,1280]{1,0:T(8,128)(2,1)} %param.40) | copy-start | bytes 4915204
  6.5 3.3 copy-start.16
  6.5 29.6 %all-reduce.28.cloned.1.call-start = ((), (), s32[]{:S(2)}) async-start(), calls=%async_computation.13 | async-start | bytes 393216 | tf_op jit(solution)/shard_map/psum | solution.py:41
  7.8 3.8 copy-start.6
  7.8 4.0 copy-start.44
  7.8 4.0 copy-start.41
  7.9 4.4 copy-start.31
  7.9 4.4 copy-start.34
  7.9 10.6 %copy-start.47 = (s32[12]{0:T(128)S(1)}, s32[12]{0:T(128)}, u32[]{:S(2)}) copy-start(s32[12]{0:T(128)} %param.25) | copy-start | bytes 148
  10.8 55.7 %all-gather.6.cloned.1.call-start = ((), (), s32[]{:S(2)}) async-start(), calls=%async_computation.5 | async-start | bytes 2359296 | tf_op jit(solution)/shard_map/all_gather | solution.py:124
  11.5 112.7 %all-gather.8.cloned.1.call-start = ((), (), s32[]{:S(2)}) async-start(), calls=%async_computation.7 | async-start | bytes 2359296 | tf_op jit(solution)/shard_map/all_gather | solution.py:124
  11.8 52.8 %copy-start.32 = (f32[1,2,4,128]{3,1,2,0:T(2,128)}, f32[1,2,4,128]{3,1,2,0:T(2,128)S(1)}, u32[]{:S(2)}) copy-start(f32[1,2,4,128]{3,1,2,0:T(2,128)S(1)} %copy.245) | copy-start | bytes 12292
  71.1 87.1 %all-gather.4.cloned.1.call-start = ((), (), s32[]{:S(2)}) async-start(), calls=%async_computation.3 | async-start | bytes 5570560 | tf_op jit(solution)/shard_map/all_gather | solution.py:94
  71.6 100.7 %reduce-scatter.4.cloned.1.call-start = ((), (), s32[]{:S(2)}) async-start(), calls=%async_computation.4 | async-start | bytes 393216 | tf_op jit(solution)/shard_map/reduce_scatter | solution.py:98
  76.3 3.5 copy-start.52
  76.3 5.4 copy-start.50
  76.3 6.1 copy-start.49
  82.4 33.9 %copy-start.35 = (pred[8,64]{1,0:T(8,128)(4,1)}, pred[8,64]{1,0:T(8,128)(4,1)S(1)}, u32[]{:S(2)}) copy-start(pred[8,64]{1,0:T(8,128)(4,1)S(1)} %broadcast_compare_fusion) | copy-start | bytes 1540
  83.1 41.0 %copy-start.24 = (pred[12,8,4,4]{0,1,3,2:T(8,128)(4,1)}, pred[12,8,4,4]{0,1,3,2:T(8,128)(4,1)S(1)}, u32[]{:S(2)}) copy-start(pred[12,8,4,4]{0,1,3,2:T(8,128)(4,1)S(1)} %get-tuple-element.72) | copy-start | bytes 4612
  116.4 3.4 copy-start.1
  123.2 5.0 copy-start.15
  123.2 5.0 copy-start.39
  123.2 5.0 copy-start.40
  124.3 33.9 %copy-start.17 = (bf16[32,1280]{1,0:T(8,128)(2,1)S(1)}, bf16[32,1280]{1,0:T(8,128)(2,1)}, u32[]{:S(2)}) copy-start(bf16[32,1280]{1,0:T(8,128)(2,1)} %reshape.371) | copy-start | bytes 245764
  162.4 135.2 %reduce-scatter.6.cloned.1.call-start = ((), (), s32[]{:S(2)}) async-start(), calls=%async_computation.6 | async-start | bytes 835584 | tf_op jit(solution)/shard_map/reduce_scatter | solution.py:185
  164.5 2.9 copy-start.22
  164.5 7.9 %copy-start.46 = (f32[16]{0:T(128)S(1)}, f32[16]{0:T(128)}, u32[]{:S(2)}) copy-start(f32[16]{0:T(128)} %fusion.118) | copy-start | bytes 196
  166.6 7.1 %copy-start.33 = (f32[1,2,4,128]{3,1,2,0:T(2,128)S(1)}, f32[1,2,4,128]{3,1,2,0:T(2,128)}, u32[]{:S(2)}) copy-start(f32[1,2,4,128]{3,1,2,0:T(2,128)} %copy-done.32) | copy-start | bytes 12292
  167.5 6.4 %copy-start.42 = (pred[4,4]{1,0:T(4,128)(4,1)S(1)}, pred[4,4]{1,0:T(4,128)(4,1)}, u32[]{:S(2)}) copy-start(pred[4,4]{1,0:T(4,128)(4,1)} %broadcast_compare_fusion.1) | copy-start | bytes 52
  167.5 10.3 %copy-start.29 = (f32[8,8,4,2]{1,3,2,0:T(2,128)S(1)}, f32[8,8,4,2]{1,3,2,0:T(2,128)}, u32[]{:S(2)}) copy-start(f32[8,8,4,2]{1,3,2,0:T(2,128)} %get-tuple-element.78) | copy-start | bytes 6148
  167.5 10.4 %copy-start.28 = (f32[8,8,4,2]{1,3,2,0:T(2,128)S(1)}, f32[8,8,4,2]{1,3,2,0:T(2,128)}, u32[]{:S(2)}) copy-start(f32[8,8,4,2]{1,3,2,0:T(2,128)} %get-tuple-element.74) | copy-start | bytes 6148
  173.8 50.0 %copy-start.12 = (f32[8,8,4,2,64]{4,1,3,2,0:T(8,128)S(1)}, f32[8,8,4,2,64]{4,1,3,2,0:T(8,128)}, u32[]{:S(2)}) copy-start(f32[8,8,4,2,64]{4,1,3,2,0:T(8,128)} %get-tuple-element.79) | copy-start | bytes 393220
  221.5 3.9 copy-start.7
  226.8 3.2 copy-start.11
  226.8 116.6 %reduce-scatter.8.cloned.1.call-start = ((), (), s32[]{:S(2)}) async-start(), calls=%async_computation.8 | async-start | bytes 835584 | tf_op jit(solution)/shard_map/reduce_scatter | solution.py:185
  231.7 2.6 copy-start.13
  231.7 2.6 copy-start.27
  231.7 2.6 copy-start.36
  233.1 133.0 %copy-start.10 = (bf16[128,1280]{1,0:T(8,128)(2,1)S(1)}, bf16[128,1280]{1,0:T(8,128)(2,1)}, u32[]{:S(2)}) copy-start(bf16[128,1280]{1,0:T(8,128)(2,1)} %param.35) | copy-start | bytes 983044
  233.1 133.0 %all-reduce.24.cloned.1.call-start = ((), (), s32[]{:S(2)}) async-start(), calls=%async_computation.11 | async-start | bytes 198656 | tf_op jit(solution)/shard_map/psum | solution.py:188
  343.5 120.4 %all-reduce.22.cloned.1.call-start = ((), (), s32[]{:S(2)}) async-start(), calls=%async_computation.10 | async-start | bytes 1966080 | tf_op jit(solution)/shard_map/psum | solution.py:191
  367.9 103.3 %copy-start.37 = (f32[1280]{0:T(1024)S(1)}, f32[1280]{0:T(1024)}, u32[]{:S(2)}) copy-start(f32[1280]{0:T(1024)} %param.36) | copy-start | bytes 15364
  369.8 103.1 %copy-start.2 = (bf16[1280,640]{1,0:T(8,128)(2,1)S(1)}, bf16[1280,640]{1,0:T(8,128)(2,1)}, u32[]{:S(2)}) copy-start(bf16[1280,640]{1,0:T(8,128)(2,1)} %param.39) | copy-start | bytes 4915204
  369.8 103.1 %copy-start.26 = (f32[1280]{0:T(1024)S(1)}, f32[1280]{0:T(1024)}, u32[]{:S(2)}) copy-start(f32[1280]{0:T(1024)} %param.37) | copy-start | bytes 15364
  369.9 145.9 %all-reduce.26.cloned.1.call-start = ((), (), s32[]{:S(2)}) async-start(), calls=%async_computation.12 | async-start | bytes 1966080 | tf_op jit(solution)/shard_map/psum | solution.py:200
  471.2 2.9 copy-start.3
  477.4 135.4 %all-reduce.20.cloned.1.call-start = ((), (), s32[]{:S(2)}) async-start(), calls=%async_computation.9 | async-start | bytes 1966080 | tf_op jit(solution)/shard_map/psum | solution.py:207
  519.4 100.6 %copy-start.38 = (f32[1280]{0:T(1024)S(1)}, f32[1280]{0:T(1024)}, u32[]{:S(2)}) copy-start(f32[1280]{0:T(1024)} %param.41) | copy-start | bytes 15364
  (16 other events, 32.0 us)
Sparse Core Ops, SparseCore 0:
  10.9 25.1 all-reduce.27
  37.6 27.1 all-gather.5
  71.2 25.6 all-gather.7
  98.9 59.2 all-gather.3
  162.5 9.8 reduce-scatter.3
  227.0 57.3 reduce-scatter.5
  287.9 55.5 reduce-scatter.7
  346.1 19.9 all-reduce.23
  370.0 93.8 all-reduce.21
  477.5 38.1 all-reduce.25
  519.6 93.1 all-reduce.19
where the time goes:
time: 630 us; the launch traced here: 629 us
  waiting for transfers between devices  340 us (54%)
  blocking collectives  167 us (27%)
  local copies, waits for them, and re-layouts  40.9 us (6%)
  matrix products  38.3 us (6%)
  other arithmetic  27.2 us (4%)
  between operations  14.9 us (2%)
    psum x1, waiting for transfers between devices, shards(): out_proj = lax.psum(partial_out, 'seq')  94 us
    psum x1, waiting for transfers between devices, shards(): lax.psum(jnp.dot(inner, w_down, preferred_element_type=f32), 'seq')  93.3 us
    unnamed x1, blocking collectives  60.1 us
    reduce_scatter x2, waiting for transfers between devices, shards(): lax.psum_scatter(weighted, 'seq', scatter_dimension=1, tiled=True)  45.9 us
    pmax x1, blocking collectives, shards(): top = lax.pmax(top, ('seq', 'head'))  40.8 us
    psum x1, waiting for transfers between devices, shards(): lax.psum((gate_part, up_part, jnp.sum(state_f * state_f, -1)), 'head')  33.1 us
    all_gather x1, waiting for transfers between devices, shards(): lax.all_gather(w_keyval, 'seq', axis=1, tiled=True)  28 us
    all_gather x1, blocking collectives, project_tokens(): lax.all_gather(kv_raw, 'seq', axis=1, tiled=True)  23.5 us
  transfers between devices with their start and end apart: 11, of which 8 were waited for; matrix products, arithmetic and copies ran while one was open for 9% of the time, Pallas kernels for 0%

commit v1 on v0

--- a/solution.py
+++ b/solution.py
@@ -204,7 +204,9 @@
         inner = (jax.nn.gelu(gate_part * norm_s, approximate=True) * (up_part * norm_s)).astype(
             bf16
         )
-        ffn_out = lax.psum(jnp.dot(inner, w_down, preferred_element_type=f32), "seq")
+        ffn_out = jnp.sum(
+            lax.all_gather(jnp.dot(inner, w_down, preferred_element_type=f32), "seq"), axis=0
+        )
         ffn_sq = lax.psum(jnp.sum(ffn_out * ffn_out, -1), "head")
         result = (state_f + ffn_out * lax.rsqrt(ffn_sq / D + EPS)[:, None] * final_gain).astype(
             bf16

time: 630 us -> 681 us (1.081)
  waiting for transfers between devices: 340 us -> 383 us
    all_gather x0 -> x2, waiting for transfers between devices: none -> 139 us  [shards(): lax.all_gather(jnp.dot(inner, w_down, preferred_element_type=f32), 'seq')]
    psum x1 -> x0, waiting for transfers between devices: 93.3 us -> none  [shards(): lax.psum(jnp.dot(inner, w_down, preferred_element_type=f32), 'seq')]
    reduce_sum x0 -> x2, other arithmetic: none -> 7.33 us  [shards(): jnp.sum(lax.all_gather(jnp.dot(inner, w_down, preferred_element_type=f32)...]
  transfers between devices with their start and end apart: 11 -> 12, of which waited for: 8 -> 9; matrix products, arithmetic and copies ran while one was open for 9% -> 10% of each run, Pallas kernels for 0% -> 0%
where the time goes in v1:
time: 681 us; the launch traced here: 679 us
  waiting for transfers between devices  383 us (56%)
  blocking collectives  167 us (25%)
  local copies, waits for them, and re-layouts  44.6 us (7%)
  matrix products  37.1 us (5%)
  other arithmetic  32.2 us (5%)
  between operations  15.2 us (2%)
    all_gather x2, waiting for transfers between devices, shards(): lax.all_gather(jnp.dot(inner, w_down, preferred_element_type=f32), 'seq')  139 us
    psum x1, waiting for transfers between devices, shards(): out_proj = lax.psum(partial_out, 'seq')  94 us
    unnamed x1, blocking collectives  60 us
    reduce_scatter x2, waiting for transfers between devices, shards(): lax.psum_scatter(weighted, 'seq', scatter_dimension=1, tiled=True)  46.2 us
    pmax x1, blocking collectives, shards(): top = lax.pmax(top, ('seq', 'head'))  40.8 us
    psum x1, waiting for transfers between devices, shards(): lax.psum((gate_part, up_part, jnp.sum(state_f * state_f, -1)), 'head')  33.1 us
    all_gather x1, waiting for transfers between devices, shards(): lax.all_gather(w_keyval, 'seq', axis=1, tiled=True)  27.8 us
    all_gather x1, blocking collectives, project_tokens(): lax.all_gather(kv_raw, 'seq', axis=1, tiled=True)  23.5 us
  transfers between devices with their start and end apart: 12, of which 9 were waited for; matrix products, arithmetic and copies ran while one was open for 10% of the time, Pallas kernels for 0%

profile of v1, /device:TPU:0, one launch (start us, length us, event | category | flops | bytes accessed | tf_op | source)
XLA Modules:
  0.0 679.4 jit_solution(2569992698711636921)
XLA Ops:
  7.9 1.9 fusion.145
  12.6 5.8 all-reduce.10
  19.1 17.0 %all-reduce.24.cloned.1.call-done = (f32[192,128]{1,0:T(8,128)}, f32[192,128]{1,0:T(8,128)}) async-done(((f32[192,128]{1,0:T(8,128)}, f32[192,128]{1,0:T(8,128)}), (f32[192,128]{1,0:T(8,128)}, f32[192,128]{1,0:T(8,128)})) %all-reduce.24.cloned.1.call-update) | async-done | bytes 196624 | tf_op jit(solution)/shard_map/psum | solution.py:41
  37.1 23.5 %all_gather.29 = bf16[192,2048]{1,0:T(8,128)(2,1)S(1)} all-gather(bf16[192,128]{1,0:T(8,128)(2,1)S(1)} %get-tuple-element.68), channel_id=1, replica_groups=mesh['seq'=16,'head'=2] {'seq'}, dimensions={1}, use_global_device_ids=true | all-gather | bytes 835584 | tf_op jit(solution)/shard_map/all_gather | solution.py:47
  62.4 1.5 mul.381
  66.5 2.9 gather_fusion
  69.4 1.6 select_select_fusion.1
  73.4 2.7 fusion.131
  76.2 1.7 reshape.377
  77.9 1.9 reshape.375
  83.2 22.2 %all_gather.28 = bf16[192,2048]{1,0:T(8,128)(2,1)S(1)} all-gather(bf16[192,128]{1,0:T(8,128)(2,1)S(1)} %get-tuple-element.69), channel_id=1, replica_groups=mesh['seq'=16,'head'=2] {'seq'}, dimensions={1}, use_global_device_ids=true | all-gather | bytes 835584 | tf_op jit(solution)/shard_map/all_gather | solution.py:46
  105.6 1.8 copy.246
  107.3 2.4 reduce_sum.198
  114.7 1.7 fusion.139
  116.5 1.7 fusion.141
  121.3 2.1 fusion.37
  124.5 3.9 gather_fusion.1
  128.4 1.9 select_select_fusion
  130.3 27.8 %all-gather.8.cloned.1.call-done = bf16[1280,2048]{1,0:T(8,128)(2,1)} async-done(((bf16[1280,128]{1,0:T(8,128)(2,1)}), bf16[1280,2048]{1,0:T(8,128)(2,1)}) %all-gather.8.cloned.1.call-update) | async-done | bytes 5242896 | tf_op jit(solution)/shard_map/all_gather | solution.py:94
  158.1 4.2 fusion.143
  162.4 1.3 fusion.133
  164.8 2.9 fusion.34
  167.7 2.0 copy.201
  170.5 1.9 reduce-scatter.4.cloned.1.call-done
  173.8 1.3 fusion.142
  175.1 1.3 fusion.140
  178.1 40.8 %all-reduce.3 = (f32[12,8,4,2]{1,3,2,0:T(2,128)S(1)}, f32[12,8,4,2]{1,3,2,0:T(2,128)S(1)}) all-reduce(f32[12,8,4,2]{1,3,2,0:T(2,128)S(1)} %maximum_maximum_fusion.1, f32[12,8,4,2]{1,3,2,0:T(2,128)S(1)} %maximum_maximum_fusion), channel_id=1, replica_groups=mesh['seq'=16,'head'=2] {'seq','head'}, use_global_device_ids=true, to_apply=%region_35.37 | all-reduce | flops 1536 | bytes 12288 | tf_op jit(solution)/shard_map/pmax | solution.py:152
  220.8 1.5 fusion.27
  224.5 1.7 convolution_bitcast_fusion.3
  226.2 1.4 fusion.4
  230.5 1.5 convolution_bitcast_fusion.2
  232.2 1.4 fusion.3
  235.6 60.0 %all-reduce.4 = (f32[96,16]{0,1:T(8,128)S(1)}, f32[96,16]{0,1:T(8,128)S(1)}) all-reduce(f32[96,16]{0,1:T(8,128)S(1)} %get-tuple-element.7, f32[96,16]{0,1:T(8,128)S(1)} %get-tuple-element.6), channel_id=9, replica_groups=mesh['seq'=16,'head'=2] {'seq'}, use_global_device_ids=true, to_apply=%region_42.44.clone | all-reduce | flops 3072 | bytes 24576
  298.0 46.2 %reduce-scatter.8.cloned.1.call-done = f32[96,128]{1,0:T(8,128)} async-done(((f32[96,2048]{1,0:T(8,128)}), f32[96,128]{1,0:T(8,128)}) %reduce-scatter.8.cloned.1.call-update) | async-done | bytes 49168 | tf_op jit(solution)/shard_map/reduce_scatter | solution.py:185
  344.3 22.5 %all-reduce.20.cloned.1.call-done = (f32[96,128]{1,0:T(8,128)}, f32[96]{0:T(128)}, f32[96,128]{1,0:T(8,128)}, f32[96]{0:T(128)}) async-done(((f32[96,128]{1,0:T(8,128)}, f32[96]{0:T(128)}, f32[96,128]{1,0:T(8,128)}, f32[96]{0:T(128)}), (f32[96,128]{1,0:T(8,128)}, f32[96]{0:T(128)}, f32[96,128]{1,0:T(8,128)}, f32[96]{0:T(128)})) %all-reduce.20.cloned.1.call-update) | async-done | bytes 99088 | tf_op jit(solution)/shard_map/psum | solution.py:188
  366.7 1.9 fusion.111
  368.6 1.9 fusion.110
  370.6 94.0 %all-reduce.18.cloned.1.call-done = (f32[96,1280]{1,0:T(8,128)}, f32[96,1280]{1,0:T(8,128)}) async-done(((f32[96,1280]{1,0:T(8,128)}, f32[96,1280]{1,0:T(8,128)}), (f32[96,1280]{1,0:T(8,128)}, f32[96,1280]{1,0:T(8,128)})) %all-reduce.18.cloned.1.call-update) | async-done | bytes 983056 | tf_op jit(solution)/shard_map/psum | solution.py:191
  466.9 4.9 all-reduce.8
  471.9 1.7 fusion.25
  478.4 4.9 all-reduce.7
  483.3 33.1 %all-reduce.22.cloned.1.call-done = (f32[96,640]{1,0:T(8,128)}, f32[96,640]{1,0:T(8,128)}, f32[96,640]{1,0:T(8,128)}, f32[96,640]{1,0:T(8,128)}) async-done(((f32[96,640]{1,0:T(8,128)}, f32[96,640]{1,0:T(8,128)}, f32[96,640]{1,0:T(8,128)}, f32[96,640]{1,0:T(8,128)}), (f32[96,640]{1,0:T(8,128)}, f32[96,640]{1,0:T(8,128)}, f32[96,640]{1,0:T(8,128)}, f32[96,640]{1,0:T(8,128)})) %all-reduce.22.cloned.1.call-update) | async-done | bytes 983056 | tf_op jit(solution)/shard_map/psum | solution.py:200
  516.4 2.4 fusion.83
  520.2 70.3 %all-gather.14.cloned.1.call-done = f32[1536,1280]{1,0:T(8,128)} async-done(((f32[96,1280]{1,0:T(8,128)}), f32[1536,1280]{1,0:T(8,128)}) %all-gather.14.cloned.1.call-update) | async-done | bytes 7864336 | tf_op jit(solution)/shard_map/all_gather | solution.py:208
  590.5 3.7 reduce_sum.206
  594.2 68.4 %all-gather.16.cloned.1.call-done = f32[1536,1280]{1,0:T(8,128)} async-done(((f32[96,1280]{1,0:T(8,128)}), f32[1536,1280]{1,0:T(8,128)}) %all-gather.16.cloned.1.call-update) | async-done | bytes 7864336 | tf_op jit(solution)/shard_map/all_gather | solution.py:208
  662.6 3.7 reduce_sum.214
  666.5 4.9 all-reduce.6
  (245 shorter events, 50.6 us)
Async XLA Ops:
  6.5 509.8 %copy-start = (bf16[640,1280]{1,0:T(8,128)(2,1)S(1)}, bf16[640,1280]{1,0:T(8,128)(2,1)}, u32[]{:S(2)}) copy-start(bf16[640,1280]{1,0:T(8,128)(2,1)} %param.40) | copy-start | bytes 4915204
  6.5 3.3 copy-start.12
  6.5 29.6 %all-reduce.24.cloned.1.call-start = ((), (), s32[]{:S(2)}) async-start(), calls=%async_computation.14 | async-start | bytes 393216 | tf_op jit(solution)/shard_map/psum | solution.py:41
  7.8 3.8 copy-start.6
  7.8 4.0 copy-start.36
  7.8 4.0 copy-start.33
  7.9 4.4 copy-start.23
  7.9 4.4 copy-start.26
  7.9 10.6 %copy-start.39 = (s32[12]{0:T(128)S(1)}, s32[12]{0:T(128)}, u32[]{:S(2)}) copy-start(s32[12]{0:T(128)} %param.25) | copy-start | bytes 148
  10.8 55.7 %all-gather.10.cloned.1.call-start = ((), (), s32[]{:S(2)}) async-start(), calls=%async_computation.5 | async-start | bytes 2359296 | tf_op jit(solution)/shard_map/all_gather | solution.py:124
  11.5 113.0 %all-gather.12.cloned.1.call-start = ((), (), s32[]{:S(2)}) async-start(), calls=%async_computation.7 | async-start | bytes 2359296 | tf_op jit(solution)/shard_map/all_gather | solution.py:124
  11.8 52.8 %copy-start.24 = (f32[1,2,4,128]{3,1,2,0:T(2,128)}, f32[1,2,4,128]{3,1,2,0:T(2,128)S(1)}, u32[]{:S(2)}) copy-start(f32[1,2,4,128]{3,1,2,0:T(2,128)S(1)} %copy.245) | copy-start | bytes 12292
  71.0 87.1 %all-gather.8.cloned.1.call-start = ((), (), s32[]{:S(2)}) async-start(), calls=%async_computation.3 | async-start | bytes 5570560 | tf_op jit(solution)/shard_map/all_gather | solution.py:94
  71.6 100.7 %reduce-scatter.4.cloned.1.call-start = ((), (), s32[]{:S(2)}) async-start(), calls=%async_computation.4 | async-start | bytes 393216 | tf_op jit(solution)/shard_map/reduce_scatter | solution.py:98
  76.2 3.6 copy-start.43
  76.2 5.6 copy-start.41
  76.2 6.2 copy-start.40
  82.5 33.9 %copy-start.27 = (pred[8,64]{1,0:T(8,128)(4,1)}, pred[8,64]{1,0:T(8,128)(4,1)S(1)}, u32[]{:S(2)}) copy-start(pred[8,64]{1,0:T(8,128)(4,1)S(1)} %broadcast_compare_fusion) | copy-start | bytes 1540
  83.2 41.1 %copy-start.18 = (pred[12,8,4,4]{0,1,3,2:T(8,128)(4,1)}, pred[12,8,4,4]{0,1,3,2:T(8,128)(4,1)S(1)}, u32[]{:S(2)}) copy-start(pred[12,8,4,4]{0,1,3,2:T(8,128)(4,1)S(1)} %get-tuple-element.70) | copy-start | bytes 4612
  116.5 3.4 copy-start.1
  123.4 5.0 copy-start.31
  123.4 5.0 copy-start.32
  124.5 33.6 %copy-start.13 = (bf16[32,1280]{1,0:T(8,128)(2,1)S(1)}, bf16[32,1280]{1,0:T(8,128)(2,1)}, u32[]{:S(2)}) copy-start(bf16[32,1280]{1,0:T(8,128)(2,1)} %reshape.371) | copy-start | bytes 245764
  162.3 135.7 %reduce-scatter.6.cloned.1.call-start = ((), (), s32[]{:S(2)}) async-start(), calls=%async_computation.6 | async-start | bytes 835584 | tf_op jit(solution)/shard_map/reduce_scatter | solution.py:185
  164.8 4.8 copy-start.16
  164.8 7.5 %copy-start.38 = (f32[16]{0:T(128)S(1)}, f32[16]{0:T(128)}, u32[]{:S(2)}) copy-start(f32[16]{0:T(128)} %fusion.118) | copy-start | bytes 196
  167.7 5.9 copy-start.25
  167.7 6.1 copy-start.34
  226.2 2.8 copy-start.17
  227.5 2.7 copy-start.35
  227.5 3.0 copy-start.9
  227.5 3.0 copy-start.28
  227.6 116.6 %reduce-scatter.8.cloned.1.call-start = ((), (), s32[]{:S(2)}) async-start(), calls=%async_computation.8 | async-start | bytes 835584 | tf_op jit(solution)/shard_map/reduce_scatter | solution.py:185
  232.1 2.5 copy-start.10
  232.1 2.5 copy-start.21
  233.5 133.2 %copy-start.8 = (bf16[128,1280]{1,0:T(8,128)(2,1)S(1)}, bf16[128,1280]{1,0:T(8,128)(2,1)}, u32[]{:S(2)}) copy-start(bf16[128,1280]{1,0:T(8,128)(2,1)} %param.35) | copy-start | bytes 983044
  233.6 133.2 %all-reduce.20.cloned.1.call-start = ((), (), s32[]{:S(2)}) async-start(), calls=%async_computation.12 | async-start | bytes 198656 | tf_op jit(solution)/shard_map/psum | solution.py:188
  344.2 120.3 %all-reduce.18.cloned.1.call-start = ((), (), s32[]{:S(2)}) async-start(), calls=%async_computation.11 | async-start | bytes 1966080 | tf_op jit(solution)/shard_map/psum | solution.py:191
  368.6 103.3 %copy-start.29 = (f32[1280]{0:T(1024)S(1)}, f32[1280]{0:T(1024)}, u32[]{:S(2)}) copy-start(f32[1280]{0:T(1024)} %param.36) | copy-start | bytes 15364
  370.5 103.1 %copy-start.2 = (bf16[1280,640]{1,0:T(8,128)(2,1)S(1)}, bf16[1280,640]{1,0:T(8,128)(2,1)}, u32[]{:S(2)}) copy-start(bf16[1280,640]{1,0:T(8,128)(2,1)} %param.39) | copy-start | bytes 4915204
  370.5 103.1 %copy-start.20 = (f32[1280]{0:T(1024)S(1)}, f32[1280]{0:T(1024)}, u32[]{:S(2)}) copy-start(f32[1280]{0:T(1024)} %param.37) | copy-start | bytes 15364
  370.5 145.9 %all-reduce.22.cloned.1.call-start = ((), (), s32[]{:S(2)}) async-start(), calls=%async_computation.13 | async-start | bytes 1966080 | tf_op jit(solution)/shard_map/psum | solution.py:200
  471.9 2.9 copy-start.3
  478.0 112.5 %all-gather.14.cloned.1.call-start = ((), (), s32[]{:S(2)}) async-start(), calls=%async_computation.9 | async-start | bytes 8355840 | tf_op jit(solution)/shard_map/all_gather | solution.py:208
  516.4 2.5 copy-start.14
  516.4 2.5 copy-start.15
  518.8 143.8 %all-gather.16.cloned.1.call-start = ((), (), s32[]{:S(2)}) async-start(), calls=%async_computation.10 | async-start | bytes 8355840 | tf_op jit(solution)/shard_map/all_gather | solution.py:208
  662.6 8.9 %copy-start.30 = (f32[1280]{0:T(1024)S(1)}, f32[1280]{0:T(1024)}, u32[]{:S(2)}) copy-start(f32[1280]{0:T(1024)} %param.41) | copy-start | bytes 15364
  (8 other events, 14.0 us)
Sparse Core Ops, SparseCore 0:
  10.9 25.1 all-reduce.23
  37.7 27.1 all-gather.9
  71.1 25.6 all-gather.11
  98.8 59.2 all-gather.7
  162.4 9.8 reduce-scatter.3
  227.7 57.3 reduce-scatter.5
  288.6 55.5 reduce-scatter.7
  346.8 19.9 all-reduce.19
  370.6 93.8 all-reduce.17
  478.1 38.1 all-reduce.21
  518.9 71.5 all-gather.13
  592.7 69.9 all-gather.15
